TPU v7x, 128 devices: a whole 4x4x4 slice. The times are simulated.
128 devices in a mesh: cp: 16 (over z, x), grp: 8 (over y, core).
Axes of the slice: x: 4, y: 4, z: 4, core: 2. Of those that a mesh axis runs over, the one named last changes fastest.
Arguments:
- queries: bfloat16 [32768, 8192], P(('cp', 'grp')), may hold values from -60 to 60
- keys: bfloat16 [32768, 1024], P(('cp', 'grp')), may hold values from -4 to 4
- values: bfloat16 [32768, 1024], P(('cp', 'grp')), may hold values from -6 to 6
- doc_lengths: int32 [16, 3], P('cp'), may hold values from 1 to 1536, 2048 in all within a row
- send_tile: int32 [128, 32], P(('cp', 'grp')), may hold values from 0 to 16, as said below
- take_slot: int32 [128, 16], P(('cp', 'grp')), may hold values from 0 to 31, as said below
Outputs:
- attended: bfloat16 [32768, 8192], P(('cp', 'grp'))
Inputs may be any that keep to these rules, and one draw needn't show every extreme that they name: `send_tile`: entry c2 * 2 + s of row d = c * 8 + g names the arrival tile (0 to 15) that device (c, g) sends in slot s to device (c2, g), and 16 marks an empty slot. Every tile of a device is sent exactly once; each device sends 2 tiles to each of exactly 8 peers and none to the others. `take_slot`: row d2 lists, for each owner tile of device d2, the received slot c * 2 + s (slot s of the tiles sent by device (c, g) of the same g) that fills it; every filled send slot fills exactly one owner tile, so each device receives from exactly 8 peers.
All inputs are finite; a program needn't handle non-finite values.
Results may differ from a plain program's by a relative error of at most 0.0037.
Values may be sent and summed in bfloat16 or wider, within the bound.
No kernel may reach another device: no remote copies, remote signals or barrier semaphores. Data moves between devices by JAX's collectives and lax.ppermute only.
A program may use at most 128 MiB of HBM per device.

v0:
```python
import functools
import math

import jax
import jax.numpy as jnp
from jax import lax
from jax.experimental import pallas as pl
from jax.experimental.pallas import tpu as pltpu
from jax.sharding import PartitionSpec as P

QUERY_HEADS = 64
KEY_VALUE_HEADS = 8
HEAD_SIZE = 128
KEY_BLOCK = 1024
LANES = 128
MASKED = -1e30


def attention_kernel(bounds, q_ref, k_ref, v_ref, *refs, previous=False):
    if previous:
        refs = refs[1:]
    o_ref, max_ref, total_ref, sum_ref = refs
    query_rows = q_ref.shape[0]
    queries_per_group = q_ref.shape[1] // HEAD_SIZE
    exp2_scale = math.log2(math.e) / math.sqrt(HEAD_SIZE)
    first_query = bounds[0]
    ends = [bounds[5], bounds[6], bounds[7]]

    query_pos = first_query + lax.broadcasted_iota(jnp.int32, (query_rows, 1), 0)
    query_start = jnp.zeros((query_rows, 1), jnp.int32)
    for end in ends:
        query_start = jnp.maximum(query_start, jnp.where(query_pos >= end, end, 0))

    max_ref[...] = jnp.full(max_ref.shape, MASKED, jnp.float32)
    total_ref[...] = jnp.zeros(total_ref.shape, jnp.float32)
    sum_ref[...] = jnp.zeros(sum_ref.shape, jnp.float32)

    def body(block, carry, masked):
        start = pl.multiple_of(block * KEY_BLOCK, KEY_BLOCK)
        key = k_ref[pl.ds(start, KEY_BLOCK), :]
        value = v_ref[pl.ds(start, KEY_BLOCK), :]
        if masked:
            key_pos = start + lax.broadcasted_iota(jnp.int32, (1, KEY_BLOCK), 1)
            allowed = (key_pos >= query_start) & (key_pos <= query_pos)
        for head in range(queries_per_group):
            query = q_ref[:, head * HEAD_SIZE:(head + 1) * HEAD_SIZE]
            scores = lax.dot_general(
                query, key, (((1,), (1,)), ((), ())), preferred_element_type=jnp.float32
            ) * exp2_scale
            if masked:
                scores = jnp.where(allowed, scores, MASKED)
            row_max = max_ref[head]
            new_max = jnp.maximum(row_max, jnp.max(scores, axis=1, keepdims=True))
            rescale = jnp.exp2(row_max - new_max)
            weights = jnp.exp2(scores - jnp.tile(new_max, (1, KEY_BLOCK // LANES)))
            total_ref[head] = rescale * total_ref[head] + jnp.sum(weights, axis=1, keepdims=True)
            sum_ref[head] = rescale * sum_ref[head] + jnp.dot(
                weights.astype(jnp.bfloat16), value, preferred_element_type=jnp.float32
            )
            max_ref[head] = new_max
        return carry

    masked_body = functools.partial(body, masked=True)
    lax.fori_loop(bounds[1], bounds[2], masked_body, 0)
    lax.fori_loop(bounds[2], bounds[3], functools.partial(body, masked=False), 0)
    lax.fori_loop(bounds[3], bounds[4], masked_body, 0)
    for head in range(queries_per_group):
        o_ref[:, head * HEAD_SIZE:(head + 1) * HEAD_SIZE] = (
            sum_ref[head] / total_ref[head]
        ).astype(o_ref.dtype)


def attention(bounds, own_queries, all_kv, head_offset, previous=None, interpret=False):
    tok_rows = own_queries.shape[0]
    group_length = all_kv.shape[0]
    kv_heads = all_kv.shape[1] // (2 * HEAD_SIZE)
    head_width = QUERY_HEADS // KEY_VALUE_HEADS * HEAD_SIZE
    call_heads = own_queries.shape[1] // head_width
    queries_per_group = head_width // HEAD_SIZE
    in_specs = [
        pl.BlockSpec((tok_rows, head_width), lambda h, b: (0, h)),
        pl.BlockSpec((group_length, HEAD_SIZE), lambda h, b: (0, h + head_offset)),
        pl.BlockSpec((group_length, HEAD_SIZE), lambda h, b: (0, h + head_offset + kv_heads)),
    ]
    operands = [bounds, own_queries, all_kv, all_kv]
    aliases = {}
    if previous is not None:
        in_specs.append(pl.BlockSpec(memory_space=pl.ANY))
        operands.append(previous)
        aliases = {4: 0}
    return pl.pallas_call(
        attention_kernel if previous is None else functools.partial(attention_kernel, previous=True),
        out_shape=jax.ShapeDtypeStruct((tok_rows, kv_heads * head_width), own_queries.dtype),
        grid_spec=pltpu.PrefetchScalarGridSpec(
            num_scalar_prefetch=1,
            grid=(call_heads,),
            in_specs=in_specs,
            out_specs=pl.BlockSpec((tok_rows, head_width), lambda h, b: (0, h + head_offset)),
            scratch_shapes=[
                pltpu.VMEM((queries_per_group, tok_rows, LANES), jnp.float32),
                pltpu.VMEM((queries_per_group, tok_rows, LANES), jnp.float32),
                pltpu.VMEM((queries_per_group, tok_rows, HEAD_SIZE), jnp.float32),
            ],
        ),
        input_output_aliases=aliases,
        cost_estimate=pl.CostEstimate(
            flops=4 * call_heads * queries_per_group * tok_rows * group_length * HEAD_SIZE,
            transcendentals=call_heads * queries_per_group * tok_rows * group_length,
            bytes_accessed=2 * own_queries.size * 2 + 2 * call_heads * group_length * HEAD_SIZE * 2,
        ),
        compiler_params=pltpu.CompilerParams(dimension_semantics=("arbitrary",)),
        interpret=interpret,
    )(*operands)


def block_bounds(doc_lengths_row, first_query, tok_rows):
    doc_ends = jnp.cumsum(doc_lengths_row).astype(jnp.int32)

    def doc_start(pos):
        return jnp.max(jnp.where(doc_ends <= pos, doc_ends, 0))

    diagonal = first_query // KEY_BLOCK
    lo_block = doc_start(first_query) // KEY_BLOCK
    full_block = (doc_start(first_query + tok_rows - 1) + KEY_BLOCK - 1) // KEY_BLOCK
    full_block = jnp.clip(full_block, lo_block, diagonal)
    hi_block = (first_query + tok_rows + KEY_BLOCK - 1) // KEY_BLOCK
    head = jnp.stack([first_query, lo_block, full_block, diagonal, hi_block]).astype(jnp.int32)
    return jnp.concatenate([head, doc_ends])


def local(queries, keys, values, doc_lengths, send_tile, take_slot):
    tok_rows = queries.shape[0]
    peer_count = lax.axis_size("cp")
    tile_rows = tok_rows // peer_count
    slot_count = send_tile.shape[1] // peer_count
    chosen = send_tile[0]
    placed = take_slot[0]

    def outgoing(source):
        tiled = source.reshape(peer_count, tile_rows, source.shape[1])
        picked = jnp.take(tiled, chosen, axis=0, mode="clip")
        return picked.reshape(peer_count * slot_count * tile_rows, source.shape[1])

    def incoming(source):
        tiled = source.reshape(peer_count * slot_count, tile_rows, source.shape[1])
        return jnp.take(tiled, placed, axis=0, mode="clip").reshape(tok_rows, source.shape[1])

    def relayout(source):
        sent = outgoing(source)
        return incoming(lax.all_to_all(sent, "cp", split_axis=0, concat_axis=0, tiled=True))

    own_kv = relayout(jnp.concatenate([keys, values], axis=1))
    all_kv = lax.all_gather(own_kv, "grp", axis=0, tiled=True)
    half = queries.shape[1] // 2
    first_queries = relayout(queries[:, :half])
    second_queries = relayout(queries[:, half:])
    member = lax.axis_index("grp")
    bounds = block_bounds(doc_lengths[0], member * tok_rows, tok_rows)
    half_heads = KEY_VALUE_HEADS // 2
    attended = attention(bounds, first_queries, all_kv, 0)
    return attention(bounds, second_queries, all_kv, half_heads, previous=attended)


def solution(mesh):
    return jax.shard_map(
        local,
        mesh=mesh,
        in_specs=(
            P(("cp", "grp"), None),
            P(("cp", "grp"), None),
            P(("cp", "grp"), None),
            P("cp", None),
            P(("cp", "grp"), None),
            P(("cp", "grp"), None),
        ),
        out_specs=P(("cp", "grp"), None),
        check_vma=False,
    )
```

profile of v0, /device:TPU:16, one launch (start us, length us, event | category | flops | bytes accessed | tf_op | source)
XLA Modules:
  0.0 273.9 jit_solution(1247242725455314083)
XLA Ops:
  6.5 0.7 pad_clamp_fusion.1
  7.2 1.3 pad_maximum_fusion
  8.5 2.0 gather_fusion.2
  10.5 0.0 copy-start
  10.5 8.0 %all-to-all-start.1 = ((bf16[16,32,2048]{2,1,0:T(8,128)(2,1)}), bf16[16,32,2048]{2,1,0:T(8,128)(2,1)S(1)}, u32[]{:S(2)}, u32[]{:S(2)}) async-start(bf16[16,32,2048]{2,1,0:T(8,128)(2,1)} %bitcast.14), calls=%async_computation.1 | async-start | bytes 4194304 | tf_op jit(solution)/shard_map/all_to_all | solution.py:150
  18.5 0.0 all-gather.2.cloned.1.call-start
  18.5 0.0 copy-done
  18.6 31.7 %all-to-all-done.1 = bf16[16,32,2048]{2,1,0:T(8,128)(2,1)S(1)} async-done(((bf16[16,32,2048]{2,1,0:T(8,128)(2,1)}), bf16[16,32,2048]{2,1,0:T(8,128)(2,1)S(1)}, u32[]{:S(2)}, u32[]{:S(2)}) %all-to-all-start.1) | async-done | bytes 2097184 | tf_op jit(solution)/shard_map/all_to_all | solution.py:150
  50.3 1.6 gather_fusion.3
  51.9 0.0 all-gather.2.cloned.1.call-update
  51.9 4.0 %fusion.2 = (bf16[256,4096]{1,0:T(8,128)(2,1)S(1)}, bf16[256,4096]{1,0:T(8,128)(2,1)}) fusion(bf16[256,8192]{1,0:T(8,128)(2,1)} %param.6), kind=kLoop, calls=%fused_computation.13 | loop fusion | bytes 8388608 | tf_op jit(solution)/shard_map/slice | solution.py:155
  55.9 4.4 %gather_fusion = bf16[32,16,4096]{2,1,0:T(8,128)(2,1)} fusion(bf16[16,16,4096]{2,1,0:T(8,128)(2,1)} %bitcast.24, s32[1024]{0:T(1024)S(1)} %pad_clamp_fusion.1), kind=kCustom, calls=%fused_computation | custom fusion | bytes 8388736 | tf_op jit(solution)/shard_map/jit(_take)/gather | solution.py:141
  60.3 4.6 %all-to-all-start = ((bf16[16,32,4096]{2,1,0:T(8,128)(2,1)}), bf16[16,32,4096]{2,1,0:T(8,128)(2,1)}, u32[]{:S(2)}, u32[]{:S(2)}) async-start(bf16[16,32,4096]{2,1,0:T(8,128)(2,1)} %bitcast.26), calls=%async_computation | async-start | bytes 8388608 | tf_op jit(solution)/shard_map/all_to_all | solution.py:150
  64.9 2.8 %gather_fusion.4 = bf16[32,16,4096]{2,1,0:T(8,128)(2,1)} fusion(bf16[16,16,4096]{2,1,0:T(8,128)(2,1)S(1)} %bitcast.23, s32[1024]{0:T(1024)S(1)} %pad_clamp_fusion.1), kind=kCustom, calls=%fused_computation.4 | custom fusion | bytes 8388736 | tf_op jit(solution)/shard_map/jit(_take)/gather | solution.py:141
  67.6 58.1 %all-to-all-done = bf16[16,32,4096]{2,1,0:T(8,128)(2,1)} async-done(((bf16[16,32,4096]{2,1,0:T(8,128)(2,1)}), bf16[16,32,4096]{2,1,0:T(8,128)(2,1)}, u32[]{:S(2)}, u32[]{:S(2)}) %all-to-all-start) | async-done | bytes 4194336 | tf_op jit(solution)/shard_map/all_to_all | solution.py:150
  125.8 0.0 copy-start.1
  125.8 4.8 %all-to-all-start.2 = ((bf16[16,32,4096]{2,1,0:T(8,128)(2,1)}), bf16[16,32,4096]{2,1,0:T(8,128)(2,1)}, u32[]{:S(2)}, u32[]{:S(2)}) async-start(bf16[16,32,4096]{2,1,0:T(8,128)(2,1)} %bitcast.25), calls=%async_computation.2 | async-start | bytes 8388608 | tf_op jit(solution)/shard_map/all_to_all | solution.py:150
  130.5 0.0 copy-done.1
  130.5 0.2 reduce-window.9
  130.7 0.7 fusion.1
  134.5 0.7 concatenate.6.bounds
  135.2 4.2 %gather_fusion.1 = bf16[16,16,4096]{2,1,0:T(8,128)(2,1)} fusion(bf16[32,16,4096]{2,1,0:T(8,128)(2,1)} %bitcast.10, s32[1024]{0:T(1024)S(1)} %pad_clamp_fusion), kind=kCustom, calls=%fused_computation.1 | custom fusion | bytes 4194368 | tf_op jit(solution)/shard_map/jit(_take)/gather | solution.py:146
  139.4 49.4 %all-to-all-done.2 = bf16[16,32,4096]{2,1,0:T(8,128)(2,1)} async-done(((bf16[16,32,4096]{2,1,0:T(8,128)(2,1)}), bf16[16,32,4096]{2,1,0:T(8,128)(2,1)}, u32[]{:S(2)}, u32[]{:S(2)}) %all-to-all-start.2) | async-done | bytes 4194336 | tf_op jit(solution)/shard_map/all_to_all | solution.py:150
  188.8 4.2 %gather_fusion.5 = bf16[16,16,4096]{2,1,0:T(8,128)(2,1)} fusion(bf16[32,16,4096]{2,1,0:T(8,128)(2,1)} %bitcast.19, s32[1024]{0:T(1024)S(1)} %pad_clamp_fusion), kind=kCustom, calls=%fused_computation.5 | custom fusion | bytes 4194368 | tf_op jit(solution)/shard_map/jit(_take)/gather | solution.py:146
  193.0 0.0 all-gather.2.cloned.1.call-done.k_ref.v_ref
  193.0 37.0 %shard_map.64.refs_0_ = bf16[256,8192]{1,0:T(8,128)(2,1)} custom-call(s32[8]{0:T(128)} %concatenate.6.bounds, bf16[256,4096]{1,0:T(8,128)(2,1)} %bitcast.31, bf16[2048,2048]{1,0:T(8,128)(2,1)} %all-gather.2.cloned.1.call-done.k_ref.v_ref, bf16[2048,2048]{1,0:T(8,128)(2,1)} %all-gather.2.cloned.1.call-done.k_ref.v_ref), custom_call_target="tpu_custom_call" | custom-call | flops 8589934592 | bytes 8388608 | tf_op jit(solution)/shard_map/pallas_call | solution.py:91
  230.0 37.1 %shard_map.65 = bf16[256,8192]{1,0:T(8,128)(2,1)} custom-call(s32[8]{0:T(128)} %concatenate.6.bounds, bf16[256,4096]{1,0:T(8,128)(2,1)} %bitcast.30, bf16[2048,2048]{1,0:T(8,128)(2,1)} %all-gather.2.cloned.1.call-done.k_ref.v_ref, bf16[2048,2048]{1,0:T(8,128)(2,1)} %all-gather.2.cloned.1.call-done.k_ref.v_ref, ...), custom_call_target="tpu_custom_call", output_to_operand_aliasing={{}: (4, {})} | custom-call | flops 8589934592 | bytes 8388608 | tf_op jit(solution)/shard_map/pallas_call | solution.py:91
  (1 shorter events, 0.0 us)
Async XLA Ops:
  10.5 8.1 %copy-start = (s32[1,16]{1,0:T(1,128)S(1)}, s32[1,16]{1,0:T(1,128)}, u32[]{:S(2)}) copy-start(s32[1,16]{1,0:T(1,128)} %param.11) | copy-start | bytes 196
  10.5 39.8 %all-to-all-start.1 = ((bf16[16,32,2048]{2,1,0:T(8,128)(2,1)}), bf16[16,32,2048]{2,1,0:T(8,128)(2,1)S(1)}, u32[]{:S(2)}, u32[]{:S(2)}) async-start(bf16[16,32,2048]{2,1,0:T(8,128)(2,1)} %bitcast.14), calls=%async_computation.1 | async-start | bytes 4194304 | tf_op jit(solution)/shard_map/all_to_all | solution.py:150
  18.5 174.5 %all-gather.2.cloned.1.call-start = ((), (), s32[]{:S(2)}) async-start(), calls=%async_computation.3 | async-start | bytes 9437184 | tf_op jit(solution)/shard_map/all_gather | solution.py:153
  60.3 65.5 %all-to-all-start = ((bf16[16,32,4096]{2,1,0:T(8,128)(2,1)}), bf16[16,32,4096]{2,1,0:T(8,128)(2,1)}, u32[]{:S(2)}, u32[]{:S(2)}) async-start(bf16[16,32,4096]{2,1,0:T(8,128)(2,1)} %bitcast.26), calls=%async_computation | async-start | bytes 8388608 | tf_op jit(solution)/shard_map/all_to_all | solution.py:150
  125.8 4.8 %copy-start.1 = (s32[1,3]{1,0:T(1,128)S(1)}, s32[1,3]{1,0:T(1,128)}, u32[]{:S(2)}) copy-start(s32[1,3]{1,0:T(1,128)} %param.9) | copy-start | bytes 40
  125.8 63.0 %all-to-all-start.2 = ((bf16[16,32,4096]{2,1,0:T(8,128)(2,1)}), bf16[16,32,4096]{2,1,0:T(8,128)(2,1)}, u32[]{:S(2)}, u32[]{:S(2)}) async-start(bf16[16,32,4096]{2,1,0:T(8,128)(2,1)} %bitcast.25), calls=%async_computation.2 | async-start | bytes 8388608 | tf_op jit(solution)/shard_map/all_to_all | solution.py:150
Sparse Core Ops, SparseCore 0:
  52.0 46.3 all-gather.1
where the time goes:
time: 275 us; the launch traced here: 274 us
  waiting for transfers between devices  139 us (51%)
  Pallas kernels  74.1 us (27%)
  local copies, waits for them, and re-layouts  23.8 us (9%)
  starting transfers between devices  17.4 us (6%)
  between operations  16.6 us (6%)
  other arithmetic  2.77 us (1%)
    all_to_all x3, waiting for transfers between devices, relayout(): lax.all_to_all(sent, 'cp', split_axis=0, concat_axis=0, tiled=True)  139 us
    pallas_call x2, Pallas kernels, attention(): pl.pallas_call(attention_kernel if previous is None else functools.partia...  74.1 us
    all_to_all x3, starting transfers between devices, relayout(): lax.all_to_all(sent, 'cp', split_axis=0, concat_axis=0, tiled=True)  17.3 us
    gather x3, local copies, waits for them, and re-layouts, incoming(): jnp.take(tiled, placed, axis=0, mode='clip')  10 us
    gather x3, local copies, waits for them, and re-layouts, outgoing(): picked = jnp.take(tiled, chosen, axis=0, mode='clip')  9.17 us
  transfers between devices with their start and end apart: 4, of which 3 were waited for; matrix products, arithmetic and copies ran while one was open for 8% of the time, Pallas kernels for 0%

commit v1 on v0

--- a/solution.py
+++ b/solution.py
@@ -46,13 +46,14 @@
             query = q_ref[:, head * HEAD_SIZE:(head + 1) * HEAD_SIZE]
             scores = lax.dot_general(
                 query, key, (((1,), (1,)), ((), ())), preferred_element_type=jnp.float32
-            ) * exp2_scale
+            )
             if masked:
                 scores = jnp.where(allowed, scores, MASKED)
             row_max = max_ref[head]
-            new_max = jnp.maximum(row_max, jnp.max(scores, axis=1, keepdims=True))
+            block_max = jnp.max(scores, axis=1, keepdims=True) * exp2_scale
+            new_max = jnp.maximum(row_max, block_max)
             rescale = jnp.exp2(row_max - new_max)
-            weights = jnp.exp2(scores - jnp.tile(new_max, (1, KEY_BLOCK // LANES)))
+            weights = jnp.exp2(scores * exp2_scale - jnp.tile(new_max, (1, KEY_BLOCK // LANES)))
             total_ref[head] = rescale * total_ref[head] + jnp.sum(weights, axis=1, keepdims=True)
             sum_ref[head] = rescale * sum_ref[head] + jnp.dot(
                 weights.astype(jnp.bfloat16), value, preferred_element_type=jnp.float32

time: 275 us -> 279 us (1.015)
  Pallas kernels: 74.1 us -> 78.8 us
    pallas_call x2, Pallas kernels: 74.1 us -> 78.8 us  [attention(): pl.pallas_call(attention_kernel if previous is None else functools.partia...]
where the time goes in v1:
time: 279 us
  waiting for transfers between devices  139 us (50%)
  Pallas kernels  78.8 us (28%)
  local copies, waits for them, and re-layouts  23.8 us (9%)
  starting transfers between devices  17.4 us (6%)
  between operations  16.6 us (6%)
    all_to_all x3, waiting for transfers between devices, relayout(): lax.all_to_all(sent, 'cp', split_axis=0, concat_axis=0, tiled=True)  139 us
    pallas_call x2, Pallas kernels, attention(): pl.pallas_call(attention_kernel if previous is None else functools.partia...  78.8 us
    all_to_all x3, starting transfers between devices, relayout(): lax.all_to_all(sent, 'cp', split_axis=0, concat_axis=0, tiled=True)  17.3 us
    gather x3, local copies, waits for them, and re-layouts, incoming(): jnp.take(tiled, placed, axis=0, mode='clip')  10 us
    gather x3, local copies, waits for them, and re-layouts, outgoing(): picked = jnp.take(tiled, chosen, axis=0, mode='clip')  9.17 us
  transfers between devices with their start and end apart: 4, of which 3 were waited for; matrix products, arithmetic and copies ran while one was open for 8% of the time, Pallas kernels for 0%

profile of v1, /device:TPU:16, one launch (start us, length us, event | category | flops | bytes accessed | tf_op | source)
XLA Modules:
  0.0 278.6 jit_solution(1340803984920755426)
XLA Ops:
  6.5 0.7 pad_clamp_fusion.1
  7.2 1.3 pad_maximum_fusion
  8.5 2.0 gather_fusion.2
  10.5 0.0 copy-start
  10.5 8.0 %all-to-all-start.1 = ((bf16[16,32,2048]{2,1,0:T(8,128)(2,1)}), bf16[16,32,2048]{2,1,0:T(8,128)(2,1)S(1)}, u32[]{:S(2)}, u32[]{:S(2)}) async-start(bf16[16,32,2048]{2,1,0:T(8,128)(2,1)} %bitcast.14), calls=%async_computation.1 | async-start | bytes 4194304 | tf_op jit(solution)/shard_map/all_to_all | solution.py:151
  18.5 0.0 all-gather.2.cloned.1.call-start
  18.5 0.0 copy-done
  18.6 31.7 %all-to-all-done.1 = bf16[16,32,2048]{2,1,0:T(8,128)(2,1)S(1)} async-done(((bf16[16,32,2048]{2,1,0:T(8,128)(2,1)}), bf16[16,32,2048]{2,1,0:T(8,128)(2,1)S(1)}, u32[]{:S(2)}, u32[]{:S(2)}) %all-to-all-start.1) | async-done | bytes 2097184 | tf_op jit(solution)/shard_map/all_to_all | solution.py:151
  50.3 1.6 gather_fusion.3
  51.9 0.0 all-gather.2.cloned.1.call-update
  51.9 4.0 %fusion.2 = (bf16[256,4096]{1,0:T(8,128)(2,1)S(1)}, bf16[256,4096]{1,0:T(8,128)(2,1)}) fusion(bf16[256,8192]{1,0:T(8,128)(2,1)} %param.6), kind=kLoop, calls=%fused_computation.13 | loop fusion | bytes 8388608 | tf_op jit(solution)/shard_map/slice | solution.py:156
  55.9 4.4 %gather_fusion = bf16[32,16,4096]{2,1,0:T(8,128)(2,1)} fusion(bf16[16,16,4096]{2,1,0:T(8,128)(2,1)} %bitcast.24, s32[1024]{0:T(1024)S(1)} %pad_clamp_fusion.1), kind=kCustom, calls=%fused_computation | custom fusion | bytes 8388736 | tf_op jit(solution)/shard_map/jit(_take)/gather | solution.py:142
  60.3 4.6 %all-to-all-start = ((bf16[16,32,4096]{2,1,0:T(8,128)(2,1)}), bf16[16,32,4096]{2,1,0:T(8,128)(2,1)}, u32[]{:S(2)}, u32[]{:S(2)}) async-start(bf16[16,32,4096]{2,1,0:T(8,128)(2,1)} %bitcast.26), calls=%async_computation | async-start | bytes 8388608 | tf_op jit(solution)/shard_map/all_to_all | solution.py:151
  64.9 2.8 gather_fusion.4
  67.6 58.1 %all-to-all-done = bf16[16,32,4096]{2,1,0:T(8,128)(2,1)} async-done(((bf16[16,32,4096]{2,1,0:T(8,128)(2,1)}), bf16[16,32,4096]{2,1,0:T(8,128)(2,1)}, u32[]{:S(2)}, u32[]{:S(2)}) %all-to-all-start) | async-done | bytes 4194336 | tf_op jit(solution)/shard_map/all_to_all | solution.py:151
  125.8 0.0 copy-start.1
  125.8 4.8 %all-to-all-start.2 = ((bf16[16,32,4096]{2,1,0:T(8,128)(2,1)}), bf16[16,32,4096]{2,1,0:T(8,128)(2,1)}, u32[]{:S(2)}, u32[]{:S(2)}) async-start(bf16[16,32,4096]{2,1,0:T(8,128)(2,1)} %bitcast.25), calls=%async_computation.2 | async-start | bytes 8388608 | tf_op jit(solution)/shard_map/all_to_all | solution.py:151
  130.5 0.0 copy-done.1
  130.5 0.2 reduce-window.9
  130.7 0.7 fusion.1
  134.5 0.7 concatenate.6.bounds
  135.2 4.2 %gather_fusion.1 = bf16[16,16,4096]{2,1,0:T(8,128)(2,1)} fusion(bf16[32,16,4096]{2,1,0:T(8,128)(2,1)} %bitcast.10, s32[1024]{0:T(1024)S(1)} %pad_clamp_fusion), kind=kCustom, calls=%fused_computation.1 | custom fusion | bytes 4194368 | tf_op jit(solution)/shard_map/jit(_take)/gather | solution.py:147
  139.4 49.4 %all-to-all-done.2 = bf16[16,32,4096]{2,1,0:T(8,128)(2,1)} async-done(((bf16[16,32,4096]{2,1,0:T(8,128)(2,1)}), bf16[16,32,4096]{2,1,0:T(8,128)(2,1)}, u32[]{:S(2)}, u32[]{:S(2)}) %all-to-all-start.2) | async-done | bytes 4194336 | tf_op jit(solution)/shard_map/all_to_all | solution.py:151
  188.8 4.2 %gather_fusion.5 = bf16[16,16,4096]{2,1,0:T(8,128)(2,1)} fusion(bf16[32,16,4096]{2,1,0:T(8,128)(2,1)} %bitcast.19, s32[1024]{0:T(1024)S(1)} %pad_clamp_fusion), kind=kCustom, calls=%fused_computation.5 | custom fusion | bytes 4194368 | tf_op jit(solution)/shard_map/jit(_take)/gather | solution.py:147
  193.0 0.0 all-gather.2.cloned.1.call-done.k_ref.v_ref
  193.0 39.4 %shard_map.64.refs_0_ = bf16[256,8192]{1,0:T(8,128)(2,1)} custom-call(s32[8]{0:T(128)} %concatenate.6.bounds, bf16[256,4096]{1,0:T(8,128)(2,1)} %bitcast.31, bf16[2048,2048]{1,0:T(8,128)(2,1)} %all-gather.2.cloned.1.call-done.k_ref.v_ref, bf16[2048,2048]{1,0:T(8,128)(2,1)} %all-gather.2.cloned.1.call-done.k_ref.v_ref), custom_call_target="tpu_custom_call" | custom-call | flops 8589934592 | bytes 8388608 | tf_op jit(solution)/shard_map/pallas_call | solution.py:92
  232.3 39.4 %shard_map.65 = bf16[256,8192]{1,0:T(8,128)(2,1)} custom-call(s32[8]{0:T(128)} %concatenate.6.bounds, bf16[256,4096]{1,0:T(8,128)(2,1)} %bitcast.30, bf16[2048,2048]{1,0:T(8,128)(2,1)} %all-gather.2.cloned.1.call-done.k_ref.v_ref, bf16[2048,2048]{1,0:T(8,128)(2,1)} %all-gather.2.cloned.1.call-done.k_ref.v_ref, ...), custom_call_target="tpu_custom_call", output_to_operand_aliasing={{}: (4, {})} | custom-call | flops 8589934592 | bytes 8388608 | tf_op jit(solution)/shard_map/pallas_call | solution.py:92
  (1 shorter events, 0.0 us)
Async XLA Ops:
  10.5 8.1 %copy-start = (s32[1,16]{1,0:T(1,128)S(1)}, s32[1,16]{1,0:T(1,128)}, u32[]{:S(2)}) copy-start(s32[1,16]{1,0:T(1,128)} %param.11) | copy-start | bytes 196
  10.5 39.8 %all-to-all-start.1 = ((bf16[16,32,2048]{2,1,0:T(8,128)(2,1)}), bf16[16,32,2048]{2,1,0:T(8,128)(2,1)S(1)}, u32[]{:S(2)}, u32[]{:S(2)}) async-start(bf16[16,32,2048]{2,1,0:T(8,128)(2,1)} %bitcast.14), calls=%async_computation.1 | async-start | bytes 4194304 | tf_op jit(solution)/shard_map/all_to_all | solution.py:151
  18.5 174.5 %all-gather.2.cloned.1.call-start = ((), (), s32[]{:S(2)}) async-start(), calls=%async_computation.3 | async-start | bytes 9437184 | tf_op jit(solution)/shard_map/all_gather | solution.py:154
  60.3 65.5 %all-to-all-start = ((bf16[16,32,4096]{2,1,0:T(8,128)(2,1)}), bf16[16,32,4096]{2,1,0:T(8,128)(2,1)}, u32[]{:S(2)}, u32[]{:S(2)}) async-start(bf16[16,32,4096]{2,1,0:T(8,128)(2,1)} %bitcast.26), calls=%async_computation | async-start | bytes 8388608 | tf_op jit(solution)/shard_map/all_to_all | solution.py:151
  125.8 4.8 %copy-start.1 = (s32[1,3]{1,0:T(1,128)S(1)}, s32[1,3]{1,0:T(1,128)}, u32[]{:S(2)}) copy-start(s32[1,3]{1,0:T(1,128)} %param.9) | copy-start | bytes 40
  125.8 63.0 %all-to-all-start.2 = ((bf16[16,32,4096]{2,1,0:T(8,128)(2,1)}), bf16[16,32,4096]{2,1,0:T(8,128)(2,1)}, u32[]{:S(2)}, u32[]{:S(2)}) async-start(bf16[16,32,4096]{2,1,0:T(8,128)(2,1)} %bitcast.25), calls=%async_computation.2 | async-start | bytes 8388608 | tf_op jit(solution)/shard_map/all_to_all | solution.py:151
Sparse Core Ops, SparseCore 0:
  52.0 46.3 all-gather.1

commit v2 on v0

--- a/solution.py
+++ b/solution.py
@@ -151,14 +151,10 @@
 
     own_kv = relayout(jnp.concatenate([keys, values], axis=1))
     all_kv = lax.all_gather(own_kv, "grp", axis=0, tiled=True)
-    half = queries.shape[1] // 2
-    first_queries = relayout(queries[:, :half])
-    second_queries = relayout(queries[:, half:])
+    own_queries = relayout(queries)
     member = lax.axis_index("grp")
     bounds = block_bounds(doc_lengths[0], member * tok_rows, tok_rows)
-    half_heads = KEY_VALUE_HEADS // 2
-    attended = attention(bounds, first_queries, all_kv, 0)
-    return attention(bounds, second_queries, all_kv, half_heads, previous=attended)
+    return attention(bounds, own_queries, all_kv, 0)
 
 
 def solution(mesh):

time: 275 us -> 271 us (0.985)
  waiting for transfers between devices: 139 us -> 149 us
  local copies, waits for them, and re-layouts: 23.8 us -> 17.6 us
  starting transfers between devices: 17.4 us -> 13 us
  Pallas kernels: 74.1 us -> 71 us
    all_to_all x3 -> x2, waiting for transfers between devices: 139 us -> 149 us  [relayout(): lax.all_to_all(sent, 'cp', split_axis=0, concat_axis=0, tiled=True)]
    all_to_all x3 -> x2, starting transfers between devices: 17.3 us -> 13 us  [relayout(): lax.all_to_all(sent, 'cp', split_axis=0, concat_axis=0, tiled=True)]
    slice x1 -> x0, local copies, waits for them, and re-layouts: 3.96 us -> none  [local(): first_queries = relayout(queries[:, :half])]
    pallas_call x2 -> x1, Pallas kernels: 74.1 us -> 71 us  [attention(): pl.pallas_call(attention_kernel if previous is None else functools.partia...]
    gather x3 -> x2, local copies, waits for them, and re-layouts: 10 us -> 7.71 us  [incoming(): jnp.take(tiled, placed, axis=0, mode='clip')]
    gather x3 -> x2, local copies, waits for them, and re-layouts: 9.17 us -> 9.23 us  [outgoing(): picked = jnp.take(tiled, chosen, axis=0, mode='clip')]
  transfers between devices with their start and end apart: 4 -> 3, of which waited for: 3 -> 2; matrix products, arithmetic and copies ran while one was open for 8% -> 5% of each run, Pallas kernels for 0% -> 0%
where the time goes in v2:
time: 271 us; the launch traced here: 270 us
  waiting for transfers between devices  149 us (55%)
  Pallas kernels  71 us (26%)
  local copies, waits for them, and re-layouts  17.6 us (6%)
  between operations  16.8 us (6%)
  starting transfers between devices  13 us (5%)
  other arithmetic  2.82 us (1%)
    all_to_all x2, waiting for transfers between devices, relayout(): lax.all_to_all(sent, 'cp', split_axis=0, concat_axis=0, tiled=True)  149 us
    pallas_call x1, Pallas kernels, attention(): pl.pallas_call(attention_kernel if previous is None else functools.partia...  71 us
    all_to_all x2, starting transfers between devices, relayout(): lax.all_to_all(sent, 'cp', split_axis=0, concat_axis=0, tiled=True)  13 us
    gather x2, local copies, waits for them, and re-layouts, outgoing(): picked = jnp.take(tiled, chosen, axis=0, mode='clip')  9.23 us
    gather x2, local copies, waits for them, and re-layouts, incoming(): jnp.take(tiled, placed, axis=0, mode='clip')  7.71 us
  transfers between devices with their start and end apart: 3, of which 2 were waited for; matrix products, arithmetic and copies ran while one was open for 5% of the time, Pallas kernels for 0%

profile of v2, /device:TPU:16, one launch (start us, length us, event | category | flops | bytes accessed | tf_op | source)
XLA Modules:
  0.0 270.2 jit_solution(12444342139431866281)
XLA Ops:
  6.5 0.7 pad_clamp_fusion.1
  7.2 1.3 pad_maximum_fusion
  8.5 0.0 copy-start
  8.5 2.0 gather_fusion.2
  10.5 7.9 %all-to-all-start.1 = ((bf16[16,32,2048]{2,1,0:T(8,128)(2,1)}), bf16[16,32,2048]{2,1,0:T(8,128)(2,1)S(1)}, u32[]{:S(2)}, u32[]{:S(2)}) async-start(bf16[16,32,2048]{2,1,0:T(8,128)(2,1)} %bitcast.14), calls=%async_computation.1 | async-start | bytes 4194304 | tf_op jit(solution)/shard_map/all_to_all | solution.py:150
  18.4 0.0 all-gather.2.cloned.1.call-start
  18.4 0.0 copy-done
  18.4 31.7 %all-to-all-done.1 = bf16[16,32,2048]{2,1,0:T(8,128)(2,1)S(1)} async-done(((bf16[16,32,2048]{2,1,0:T(8,128)(2,1)}), bf16[16,32,2048]{2,1,0:T(8,128)(2,1)S(1)}, u32[]{:S(2)}, u32[]{:S(2)}) %all-to-all-start.1) | async-done | bytes 2097184 | tf_op jit(solution)/shard_map/all_to_all | solution.py:150
  50.1 1.6 gather_fusion.3
  51.7 0.0 all-gather.2.cloned.1.call-update
  51.8 7.2 %gather_fusion = bf16[32,16,8192]{2,1,0:T(8,128)(2,1)} fusion(bf16[16,16,8192]{2,1,0:T(8,128)(2,1)} %bitcast.20, s32[1024]{0:T(1024)S(1)} %pad_clamp_fusion.1), kind=kCustom, calls=%fused_computation | custom fusion | bytes 16777344 | tf_op jit(solution)/shard_map/jit(_take)/gather | solution.py:141
  59.0 0.0 copy-start.1
  59.0 5.1 %all-to-all-start = ((bf16[16,32,8192]{2,1,0:T(8,128)(2,1)}), bf16[16,32,8192]{2,1,0:T(8,128)(2,1)}, u32[]{:S(2)}, u32[]{:S(2)}) async-start(bf16[16,32,8192]{2,1,0:T(8,128)(2,1)} %bitcast.19), calls=%async_computation | async-start | bytes 16777216 | tf_op jit(solution)/shard_map/all_to_all | solution.py:150
  64.1 0.0 copy-done.1
  64.1 0.2 reduce-window.9
  64.3 0.7 fusion.1
  68.3 0.6 concatenate.6.bounds
  68.9 117.3 %all-to-all-done = bf16[16,32,8192]{2,1,0:T(8,128)(2,1)} async-done(((bf16[16,32,8192]{2,1,0:T(8,128)(2,1)}), bf16[16,32,8192]{2,1,0:T(8,128)(2,1)}, u32[]{:S(2)}, u32[]{:S(2)}) %all-to-all-start) | async-done | bytes 8388640 | tf_op jit(solution)/shard_map/all_to_all | solution.py:150
  186.2 6.1 %gather_fusion.1 = bf16[16,16,8192]{2,1,0:T(8,128)(2,1)} fusion(bf16[32,16,8192]{2,1,0:T(8,128)(2,1)} %bitcast.10, s32[1024]{0:T(1024)S(1)} %pad_clamp_fusion), kind=kCustom, calls=%fused_computation.1 | custom fusion | bytes 8388672 | tf_op jit(solution)/shard_map/jit(_take)/gather | solution.py:146
  192.3 0.0 all-gather.2.cloned.1.call-done.k_ref.v_ref
  192.3 71.0 %shard_map.64 = bf16[256,8192]{1,0:T(8,128)(2,1)} custom-call(s32[8]{0:T(128)} %concatenate.6.bounds, bf16[256,8192]{1,0:T(8,128)(2,1)} %bitcast.24, bf16[2048,2048]{1,0:T(8,128)(2,1)} %all-gather.2.cloned.1.call-done.k_ref.v_ref, bf16[2048,2048]{1,0:T(8,128)(2,1)} %all-gather.2.cloned.1.call-done.k_ref.v_ref), custom_call_target="tpu_custom_call" | custom-call | flops 17179869184 | bytes 16777216 | tf_op jit(solution)/shard_map/pallas_call | solution.py:91
  (1 shorter events, 0.0 us)
Async XLA Ops:
  8.5 9.9 %copy-start = (s32[1,16]{1,0:T(1,128)S(1)}, s32[1,16]{1,0:T(1,128)}, u32[]{:S(2)}) copy-start(s32[1,16]{1,0:T(1,128)} %param.11) | copy-start | bytes 196
  10.5 39.7 %all-to-all-start.1 = ((bf16[16,32,2048]{2,1,0:T(8,128)(2,1)}), bf16[16,32,2048]{2,1,0:T(8,128)(2,1)S(1)}, u32[]{:S(2)}, u32[]{:S(2)}) async-start(bf16[16,32,2048]{2,1,0:T(8,128)(2,1)} %bitcast.14), calls=%async_computation.1 | async-start | bytes 4194304 | tf_op jit(solution)/shard_map/all_to_all | solution.py:150
  18.4 173.9 %all-gather.2.cloned.1.call-start = ((), (), s32[]{:S(2)}) async-start(), calls=%async_computation.2 | async-start | bytes 9437184 | tf_op jit(solution)/shard_map/all_gather | solution.py:153
  59.0 5.1 %copy-start.1 = (s32[1,3]{1,0:T(1,128)S(1)}, s32[1,3]{1,0:T(1,128)}, u32[]{:S(2)}) copy-start(s32[1,3]{1,0:T(1,128)} %param.9) | copy-start | bytes 40
  59.0 127.2 %all-to-all-start = ((bf16[16,32,8192]{2,1,0:T(8,128)(2,1)}), bf16[16,32,8192]{2,1,0:T(8,128)(2,1)}, u32[]{:S(2)}, u32[]{:S(2)}) async-start(bf16[16,32,8192]{2,1,0:T(8,128)(2,1)} %bitcast.19), calls=%async_computation | async-start | bytes 16777216 | tf_op jit(solution)/shard_map/all_to_all | solution.py:150
Sparse Core Ops, SparseCore 0:
  51.9 46.3 all-gather.1

commit v3 on v2

--- a/solution.py
+++ b/solution.py
@@ -113,6 +113,75 @@
     )(*operands)
 
 
+def gathered_kernel(bounds, placed, got_hbm, k_ref, v_ref, o_ref, qbuf, sems, *state):
+    step = pl.program_id(0)
+    steps = pl.num_programs(0)
+    tiles = placed.shape[0]
+    tile_rows = qbuf.shape[1] // tiles
+    width = qbuf.shape[2]
+    slots_total = got_hbm.shape[0] // tile_rows
+
+    def fetch(target_step, slot):
+        for tile in range(tiles):
+            source_slot = jnp.clip(placed[tile], 0, slots_total - 1)
+            pltpu.make_async_copy(
+                got_hbm.at[pl.ds(source_slot * tile_rows, tile_rows), pl.ds(target_step * width, width)],
+                qbuf.at[slot, pl.ds(tile * tile_rows, tile_rows), :],
+                sems.at[slot],
+            ).start()
+
+    @pl.when(step == 0)
+    def _():
+        fetch(0, 0)
+
+    slot = step % 2
+
+    @pl.when(step + 1 < steps)
+    def _():
+        fetch(step + 1, 1 - slot)
+
+    pltpu.make_async_copy(
+        got_hbm.at[pl.ds(0, qbuf.shape[1]), pl.ds(0, width)], qbuf.at[slot], sems.at[slot]
+    ).wait()
+    attention_kernel(bounds, qbuf.at[slot], k_ref, v_ref, o_ref, *state)
+
+
+def attention_gathered(bounds, placed, got, all_kv, interpret=False):
+    tok_rows = got.shape[0] // 2
+    group_length = all_kv.shape[0]
+    kv_heads = all_kv.shape[1] // (2 * HEAD_SIZE)
+    head_width = got.shape[1] // kv_heads
+    queries_per_group = head_width // HEAD_SIZE
+    return pl.pallas_call(
+        gathered_kernel,
+        out_shape=jax.ShapeDtypeStruct((tok_rows, got.shape[1]), got.dtype),
+        grid_spec=pltpu.PrefetchScalarGridSpec(
+            num_scalar_prefetch=2,
+            grid=(kv_heads,),
+            in_specs=[
+                pl.BlockSpec(memory_space=pl.ANY),
+                pl.BlockSpec((group_length, HEAD_SIZE), lambda h, b, p: (0, h)),
+                pl.BlockSpec((group_length, HEAD_SIZE), lambda h, b, p: (0, h + kv_heads)),
+            ],
+            out_specs=pl.BlockSpec((tok_rows, head_width), lambda h, b, p: (0, h)),
+            scratch_shapes=[
+                pltpu.VMEM((2, tok_rows, head_width), got.dtype),
+                pltpu.SemaphoreType.DMA((2,)),
+                pltpu.VMEM((queries_per_group, tok_rows, LANES), jnp.float32),
+                pltpu.VMEM((queries_per_group, tok_rows, LANES), jnp.float32),
+                pltpu.VMEM((queries_per_group, tok_rows, HEAD_SIZE), jnp.float32),
+            ],
+        ),
+        cost_estimate=pl.CostEstimate(
+            flops=4 * kv_heads * queries_per_group * tok_rows * group_length * HEAD_SIZE,
+            transcendentals=kv_heads * queries_per_group * tok_rows * group_length,
+            bytes_accessed=4 * tok_rows * got.shape[1] + 2 * kv_heads * group_length * HEAD_SIZE * 2,
+        ),
+        compiler_params=pltpu.CompilerParams(dimension_semantics=("arbitrary",)),
+        interpret=interpret,
+    )(bounds, placed, got, all_kv, all_kv)
+
+
 def block_bounds(doc_lengths_row, first_query, tok_rows):
     doc_ends = jnp.cumsum(doc_lengths_row).astype(jnp.int32)
 
@@ -151,10 +220,10 @@
 
     own_kv = relayout(jnp.concatenate([keys, values], axis=1))
     all_kv = lax.all_gather(own_kv, "grp", axis=0, tiled=True)
-    own_queries = relayout(queries)
+    got_queries = lax.all_to_all(outgoing(queries), "cp", split_axis=0, concat_axis=0, tiled=True)
     member = lax.axis_index("grp")
     bounds = block_bounds(doc_lengths[0], member * tok_rows, tok_rows)
-    return attention(bounds, own_queries, all_kv, 0)
+    return attention_gathered(bounds, placed, got_queries, all_kv)
 
 
 def solution(mesh):

time: 271 us -> 266 us (0.982)
  local copies, waits for them, and re-layouts: 17.6 us -> 11.4 us
    all_to_all x2 -> x1, waiting for transfers between devices: 149 us -> 31.7 us  [relayout(): lax.all_to_all(sent, 'cp', split_axis=0, concat_axis=0, tiled=True)]
    all_to_all x0 -> x1, waiting for transfers between devices: none -> 117 us  [local(): lax.all_to_all(outgoing(queries), 'cp', split_axis=0, concat_axis=0, tile...]
    gather x2 -> x1, local copies, waits for them, and re-layouts: 7.71 us -> 1.58 us  [incoming(): jnp.take(tiled, placed, axis=0, mode='clip')]
    all_to_all x0 -> x1, starting transfers between devices: none -> 5.09 us  [local(): lax.all_to_all(outgoing(queries), 'cp', split_axis=0, concat_axis=0, tile...]
    all_to_all x2 -> x1, starting transfers between devices: 13 us -> 7.88 us  [relayout(): lax.all_to_all(sent, 'cp', split_axis=0, concat_axis=0, tiled=True)]
  transfers between devices with their start and end apart: 3 -> 3, of which waited for: 2 -> 2; matrix products, arithmetic and copies ran while one was open for 5% -> 3% of each run, Pallas kernels for 0% -> 0%
where the time goes in v3:
time: 266 us
  waiting for transfers between devices  149 us (56%)
  Pallas kernels  72.9 us (27%)
  between operations  16.8 us (6%)
  starting transfers between devices  13 us (5%)
  local copies, waits for them, and re-layouts  11.4 us (4%)
  other arithmetic  2.82 us (1%)
    all_to_all x1, waiting for transfers between devices, local(): lax.all_to_all(outgoing(queries), 'cp', split_axis=0, concat_axis=0, tile...  117 us
    pallas_call x1, Pallas kernels, attention_gathered(): pl.pallas_call(gathered_kernel, out_shape=jax.ShapeDtypeStruct((tok_rows,...  72.9 us
    all_to_all x1, waiting for transfers between devices, relayout(): lax.all_to_all(sent, 'cp', split_axis=0, concat_axis=0, tiled=True)  31.7 us
    gather x2, local copies, waits for them, and re-layouts, outgoing(): picked = jnp.take(tiled, chosen, axis=0, mode='clip')  9.23 us
    all_to_all x1, starting transfers between devices, relayout(): lax.all_to_all(sent, 'cp', split_axis=0, concat_axis=0, tiled=True)  7.88 us
  transfers between devices with their start and end apart: 3, of which 2 were waited for; matrix products, arithmetic and copies ran while one was open for 3% of the time, Pallas kernels for 0%

profile of v3, /device:TPU:16, one launch (start us, length us, event | category | flops | bytes accessed | tf_op | source)
XLA Modules:
  0.0 265.9 jit_solution(8481111010143180581)
XLA Ops:
  6.5 0.7 pad_clamp_fusion.1
  7.2 1.3 pad_maximum_fusion
  8.5 0.0 copy-start
  8.5 2.0 gather_fusion.1
  10.5 7.9 %all-to-all-start.1 = ((bf16[16,32,2048]{2,1,0:T(8,128)(2,1)}), bf16[16,32,2048]{2,1,0:T(8,128)(2,1)S(1)}, u32[]{:S(2)}, u32[]{:S(2)}) async-start(bf16[16,32,2048]{2,1,0:T(8,128)(2,1)} %bitcast.13), calls=%async_computation.1 | async-start | bytes 4194304 | tf_op jit(solution)/shard_map/all_to_all | solution.py:219
  18.4 0.0 all-gather.2.cloned.1.call-start
  18.4 0.0 copy-done
  18.4 31.7 %all-to-all-done.1 = bf16[16,32,2048]{2,1,0:T(8,128)(2,1)S(1)} async-done(((bf16[16,32,2048]{2,1,0:T(8,128)(2,1)}), bf16[16,32,2048]{2,1,0:T(8,128)(2,1)S(1)}, u32[]{:S(2)}, u32[]{:S(2)}) %all-to-all-start.1) | async-done | bytes 2097184 | tf_op jit(solution)/shard_map/all_to_all | solution.py:219
  50.1 1.6 gather_fusion.2
  51.7 0.0 all-gather.2.cloned.1.call-update
  51.8 7.2 %gather_fusion = bf16[32,16,8192]{2,1,0:T(8,128)(2,1)} fusion(bf16[16,16,8192]{2,1,0:T(8,128)(2,1)} %bitcast.19, s32[1024]{0:T(1024)S(1)} %pad_clamp_fusion.1), kind=kCustom, calls=%fused_computation | custom fusion | bytes 16777344 | tf_op jit(solution)/shard_map/jit(_take)/gather | solution.py:210
  59.0 0.0 copy-start.1
  59.0 5.1 %all-to-all-start = ((bf16[16,32,8192]{2,1,0:T(8,128)(2,1)}), bf16[16,32,8192]{2,1,0:T(8,128)(2,1)}, u32[]{:S(2)}, u32[]{:S(2)}) async-start(bf16[16,32,8192]{2,1,0:T(8,128)(2,1)} %bitcast.18), calls=%async_computation | async-start | bytes 16777216 | tf_op jit(solution)/shard_map/all_to_all | solution.py:223
  64.1 0.0 copy-done.1
  64.1 0.2 reduce-window.9
  64.3 0.7 fusion.1
  68.3 0.6 concatenate.6.bounds
  68.9 117.2 %all-to-all-done = bf16[16,32,8192]{2,1,0:T(8,128)(2,1)} async-done(((bf16[16,32,8192]{2,1,0:T(8,128)(2,1)}), bf16[16,32,8192]{2,1,0:T(8,128)(2,1)}, u32[]{:S(2)}, u32[]{:S(2)}) %all-to-all-start) | async-done | bytes 8388640 | tf_op jit(solution)/shard_map/all_to_all | solution.py:223
  186.1 0.0 all-gather.2.cloned.1.call-done.k_ref.v_ref
  186.1 72.9 %shard_map.64 = bf16[256,8192]{1,0:T(8,128)(2,1)} custom-call(s32[8]{0:T(128)} %concatenate.6.bounds, s32[16]{0:T(128)} %bitcast.25, bf16[512,8192]{1,0:T(8,128)(2,1)} %bitcast.11.got_hbm, bf16[2048,2048]{1,0:T(8,128)(2,1)} %all-gather.2.cloned.1.call-done.k_ref.v_ref, bf16[2048,2048]{1,0:T(8,128)(2,1)} %all-gather.2.cloned.1.call-done.k_ref.v_ref), custom_call_target="tpu_custom_call" | custom-call | flops 17179869184 | bytes 16777216 | tf_op jit(solution)/shard_map/pallas_call | solution.py:155
  (1 shorter events, 0.0 us)
Async XLA Ops:
  8.5 9.9 %copy-start = (s32[1,16]{1,0:T(1,128)S(1)}, s32[1,16]{1,0:T(1,128)}, u32[]{:S(2)}) copy-start(s32[1,16]{1,0:T(1,128)} %param.11) | copy-start | bytes 196
  10.5 39.7 %all-to-all-start.1 = ((bf16[16,32,2048]{2,1,0:T(8,128)(2,1)}), bf16[16,32,2048]{2,1,0:T(8,128)(2,1)S(1)}, u32[]{:S(2)}, u32[]{:S(2)}) async-start(bf16[16,32,2048]{2,1,0:T(8,128)(2,1)} %bitcast.13), calls=%async_computation.1 | async-start | bytes 4194304 | tf_op jit(solution)/shard_map/all_to_all | solution.py:219
  18.4 167.7 %all-gather.2.cloned.1.call-start = ((), (), s32[]{:S(2)}) async-start(), calls=%async_computation.2 | async-start | bytes 9437184 | tf_op jit(solution)/shard_map/all_gather | solution.py:222
  59.0 5.1 %copy-start.1 = (s32[1,3]{1,0:T(1,128)S(1)}, s32[1,3]{1,0:T(1,128)}, u32[]{:S(2)}) copy-start(s32[1,3]{1,0:T(1,128)} %param.9) | copy-start | bytes 40
  59.0 127.1 %all-to-all-start = ((bf16[16,32,8192]{2,1,0:T(8,128)(2,1)}), bf16[16,32,8192]{2,1,0:T(8,128)(2,1)}, u32[]{:S(2)}, u32[]{:S(2)}) async-start(bf16[16,32,8192]{2,1,0:T(8,128)(2,1)} %bitcast.18), calls=%async_computation | async-start | bytes 16777216 | tf_op jit(solution)/shard_map/all_to_all | solution.py:223
Sparse Core Ops, SparseCore 0:
  51.9 46.3 all-gather.1

commit v4 on v3

--- a/solution.py
+++ b/solution.py
@@ -182,6 +182,36 @@
     )(bounds, placed, got, all_kv, all_kv)
 
 
+def send_kernel(chosen, source_hbm, sent_hbm, sem):
+    slots = chosen.shape[0]
+    tile_rows = sent_hbm.shape[0] // slots
+    tiles = source_hbm.shape[0] // tile_rows
+    for slot in range(slots):
+        tile = jnp.clip(chosen[slot], 0, tiles - 1)
+        pltpu.make_async_copy(
+            source_hbm.at[pl.ds(tile * tile_rows, tile_rows), :],
+            sent_hbm.at[pl.ds(slot * tile_rows, tile_rows), :],
+            sem.at[0],
+        ).start()
+    pltpu.make_async_copy(sent_hbm, sent_hbm, sem.at[0]).wait()
+
+
+def send_buffer(chosen, source, interpret=False):
+    tile_rows = source.shape[0] // (chosen.shape[0] // 2)
+    return pl.pallas_call(
+        send_kernel,
+        out_shape=jax.ShapeDtypeStruct((chosen.shape[0] * tile_rows, source.shape[1]), source.dtype),
+        grid_spec=pltpu.PrefetchScalarGridSpec(
+            num_scalar_prefetch=1,
+            grid=(),
+            in_specs=[pl.BlockSpec(memory_space=pl.ANY)],
+            out_specs=pl.BlockSpec(memory_space=pl.ANY),
+            scratch_shapes=[pltpu.SemaphoreType.DMA((1,))],
+        ),
+        interpret=interpret,
+    )(chosen, source)
+
+
 def block_bounds(doc_lengths_row, first_query, tok_rows):
     doc_ends = jnp.cumsum(doc_lengths_row).astype(jnp.int32)
 
@@ -220,7 +250,9 @@
 
     own_kv = relayout(jnp.concatenate([keys, values], axis=1))
     all_kv = lax.all_gather(own_kv, "grp", axis=0, tiled=True)
-    got_queries = lax.all_to_all(outgoing(queries), "cp", split_axis=0, concat_axis=0, tiled=True)
+    got_queries = lax.all_to_all(
+        send_buffer(chosen, queries), "cp", split_axis=0, concat_axis=0, tiled=True
+    )
     member = lax.axis_index("grp")
     bounds = block_bounds(doc_lengths[0], member * tok_rows, tok_rows)
     return attention_gathered(bounds, placed, got_queries, all_kv)

time: 266 us -> 515 us (1.94)
  Pallas kernels: 72.9 us -> 329 us
  local copies, waits for them, and re-layouts: 11.4 us -> 4.2 us
    pallas_call x0 -> x1, Pallas kernels: none -> 256 us  [send_buffer(): pl.pallas_call(send_kernel, out_shape=jax.ShapeDtypeStruct((chosen.shape[...]
    gather x2 -> x1, local copies, waits for them, and re-layouts: 9.23 us -> 2 us  [outgoing(): picked = jnp.take(tiled, chosen, axis=0, mode='clip')]
  transfers between devices with their start and end apart: 3 -> 3, of which waited for: 2 -> 2; matrix products, arithmetic and copies ran while one was open for 3% -> 0% of each run, Pallas kernels for 0% -> 50%
where the time goes in v4:
time: 515 us
  Pallas kernels  329 us (64%)
  waiting for transfers between devices  149 us (29%)
  between operations  16.8 us (3%)
  starting transfers between devices  12.9 us (3%)
    pallas_call x1, Pallas kernels, send_buffer(): pl.pallas_call(send_kernel, out_shape=jax.ShapeDtypeStruct((chosen.shape[...  256 us
    all_to_all x1, waiting for transfers between devices, local(): lax.all_to_all(send_buffer(chosen, queries), 'cp', split_axis=0, concat_a...  117 us
    pallas_call x1, Pallas kernels, attention_gathered(): pl.pallas_call(gathered_kernel, out_shape=jax.ShapeDtypeStruct((tok_rows,...  73 us
    all_to_all x1, waiting for transfers between devices, relayout(): lax.all_to_all(sent, 'cp', split_axis=0, concat_axis=0, tiled=True)  31.7 us
  transfers between devices with their start and end apart: 3, of which 2 were waited for; matrix products, arithmetic and copies ran while one was open for 0% of the time, Pallas kernels for 50%

profile of v4, /device:TPU:16, one launch (start us, length us, event | category | flops | bytes accessed | tf_op | source)
XLA Modules:
  0.0 514.7 jit_solution(1190107598575845085)
XLA Ops:
  6.5 0.7 pad_clamp_fusion.1
  7.2 1.3 pad_maximum_fusion
  8.5 2.0 gather_fusion
  10.5 0.0 copy-start
  10.5 8.0 %all-to-all-start.1 = ((bf16[16,32,2048]{2,1,0:T(8,128)(2,1)}), bf16[16,32,2048]{2,1,0:T(8,128)(2,1)S(1)}, u32[]{:S(2)}, u32[]{:S(2)}) async-start(bf16[16,32,2048]{2,1,0:T(8,128)(2,1)} %bitcast.12), calls=%async_computation.1 | async-start | bytes 4194304 | tf_op jit(solution)/shard_map/all_to_all | solution.py:249
  18.5 0.0 all-gather.2.cloned.1.call-start
  18.5 0.0 copy-done
  18.6 31.7 %all-to-all-done.1 = bf16[16,32,2048]{2,1,0:T(8,128)(2,1)S(1)} async-done(((bf16[16,32,2048]{2,1,0:T(8,128)(2,1)}), bf16[16,32,2048]{2,1,0:T(8,128)(2,1)S(1)}, u32[]{:S(2)}, u32[]{:S(2)}) %all-to-all-start.1) | async-done | bytes 2097184 | tf_op jit(solution)/shard_map/all_to_all | solution.py:249
  50.3 1.6 gather_fusion.1
  51.9 0.0 all-gather.2.cloned.1.call-update
  51.9 255.9 %shard_map.64 = bf16[512,8192]{1,0:T(8,128)(2,1)} custom-call(s32[32]{0:T(128)} %bitcast.22, bf16[256,8192]{1,0:T(8,128)(2,1)} %source_hbm.1), custom_call_target="tpu_custom_call" | custom-call | tf_op jit(solution)/shard_map/pallas_call | solution.py:201
  307.8 0.0 copy-start.1
  307.8 4.8 all-to-all-start
  312.6 0.0 copy-done.1
  312.6 0.2 reduce-window.9
  312.8 0.7 fusion.1
  316.8 0.6 concatenate.6.bounds
  317.4 117.4 %all-to-all-done = bf16[16,32,8192]{2,1,0:T(8,128)(2,1)} async-done(((bf16[16,32,8192]{2,1,0:T(8,128)(2,1)}), bf16[16,32,8192]{2,1,0:T(8,128)(2,1)}, u32[]{:S(2)}, u32[]{:S(2)}) %all-to-all-start) | async-done | bytes 8388640 | tf_op jit(solution)/shard_map/all_to_all | solution.py:253
  434.8 0.0 all-gather.2.cloned.1.call-done.k_ref.v_ref
  434.8 73.0 %shard_map.65 = bf16[256,8192]{1,0:T(8,128)(2,1)} custom-call(s32[8]{0:T(128)} %concatenate.6.bounds, s32[16]{0:T(128)} %bitcast.24, bf16[512,8192]{1,0:T(8,128)(2,1)} %bitcast.10.got_hbm, bf16[2048,2048]{1,0:T(8,128)(2,1)} %all-gather.2.cloned.1.call-done.k_ref.v_ref, bf16[2048,2048]{1,0:T(8,128)(2,1)} %all-gather.2.cloned.1.call-done.k_ref.v_ref), custom_call_target="tpu_custom_call" | custom-call | flops 17179869184 | bytes 16777216 | tf_op jit(solution)/shard_map/pallas_call | solution.py:155
  (1 shorter events, 0.0 us)
Async XLA Ops:
  10.5 8.1 %copy-start = (s32[1,16]{1,0:T(1,128)S(1)}, s32[1,16]{1,0:T(1,128)}, u32[]{:S(2)}) copy-start(s32[1,16]{1,0:T(1,128)} %param.11) | copy-start | bytes 196
  10.5 39.8 %all-to-all-start.1 = ((bf16[16,32,2048]{2,1,0:T(8,128)(2,1)}), bf16[16,32,2048]{2,1,0:T(8,128)(2,1)S(1)}, u32[]{:S(2)}, u32[]{:S(2)}) async-start(bf16[16,32,2048]{2,1,0:T(8,128)(2,1)} %bitcast.12), calls=%async_computation.1 | async-start | bytes 4194304 | tf_op jit(solution)/shard_map/all_to_all | solution.py:249
  18.5 416.3 %all-gather.2.cloned.1.call-start = ((), (), s32[]{:S(2)}) async-start(), calls=%async_computation.2 | async-start | bytes 9437184 | tf_op jit(solution)/shard_map/all_gather | solution.py:252
  307.8 4.8 copy-start.1
  307.8 127.1 %all-to-all-start = ((bf16[16,32,8192]{2,1,0:T(8,128)(2,1)}), bf16[16,32,8192]{2,1,0:T(8,128)(2,1)}, u32[]{:S(2)}, u32[]{:S(2)}) async-start(bf16[16,32,8192]{2,1,0:T(8,128)(2,1)} %bitcast.17), calls=%async_computation | async-start | bytes 16777216 | tf_op jit(solution)/shard_map/all_to_all | solution.py:253
Sparse Core Ops, SparseCore 0:
  52.0 46.3 all-gather.1
